TPU v7x, 128 devices: a whole 4x4x4 slice. The times are simulated.
128 devices in a mesh: wide: 64 (over z, y, x), narrow: 2 (over core).
Axes of the slice: x: 4, y: 4, z: 4, core: 2. Of those that a mesh axis runs over, the one named last changes fastest.
Arguments:
- tokens: bfloat16 [65536, 2048], P('wide', 'narrow'), may hold values from -6 to 6
- attn_gain: bfloat16 [2048], replicated, may hold values from 0.5 to 1.5
- q_weight: bfloat16 [2048, 3072], P('wide', 'narrow'), may hold values from -6 to 6
- kva_weight: bfloat16 [2048, 576], P('wide'), may hold values from -0.125 to 0.125
- kv_gain: bfloat16 [512], replicated, may hold values from 0.5 to 1.5
- kvb_weight: bfloat16 [512, 4096], P(None, 'narrow'), may hold values from -0.25 to 0.25
- o_weight: bfloat16 [2048, 2048], P('narrow'), may hold values from -0.125 to 0.125
- adapter_down: bfloat16 [2048, 1024], P(None, 'narrow'), may hold values from -0.125 to 0.125
- adapter_up_weight: bfloat16 [1024, 3072], P(None, 'narrow'), may hold values from -1.5 to 1.5
- lengths: int32 [64, 4], P('wide'), may hold values from 1 to 512, 1024 in all within a row
- adapter_ids: int32 [64, 4], P('wide'), may hold values from 0 to 63
- adapter_slot: int32 [64], replicated, may hold values from 0 to 63, each once
Outputs:
- hidden: bfloat16 [65536, 2048], P('wide', 'narrow')
- latent_cache: bfloat16 [65536, 576], P('wide')
Inputs may be any that keep to these rules, and one draw needn't show every extreme that they name: Each row of lengths sums to 1024, and its longest prompt is exactly 512.
All inputs are finite; a program needn't handle non-finite values.
Results may differ from a plain program's by a relative error of at most 0.0095.
The roundings to bfloat16 on the way count: a program that leaves them out, or rounds other values in their place, can miss the bound.
Values may be sent and summed in bfloat16 or wider, within the bound.
No kernel may reach another device: no remote copies, remote signals or barrier semaphores. Data moves between devices by JAX's collectives and lax.ppermute only.
A program may use at most 192 MiB of HBM per device.

v0:
```python
import jax
import jax.numpy as jnp
from jax import lax
from jax.sharding import PartitionSpec as P

NOPE = 128
ROPE = 64
VDIM = 128
LATENT = 512
RANK = 16
EPS = 1e-06
THETA = 50000.0
ADAPTER_SCALE = 2.0


def rms_scale(values, gain):
    mean_sq = jnp.mean(values * values, axis=-1, keepdims=True)
    return values * lax.rsqrt(mean_sq + EPS) * gain.astype(jnp.float32)


def rotate(values, positions):
    half = values.shape[-1] // 2
    freqs = jnp.exp(-jnp.log(THETA) * 2.0 * jnp.arange(half).astype(jnp.float32) / (2 * half))
    angle = positions.astype(jnp.float32)[:, None] * freqs[None, :]
    cosine = jnp.cos(angle)
    sine = jnp.sin(angle)
    if values.ndim == 3:
        cosine = cosine[:, None, :]
        sine = sine[:, None, :]
    first = values[..., :half]
    second = values[..., half:]
    return jnp.concatenate(
        [first * cosine - second * sine, first * sine + second * cosine], axis=-1
    )


def token_tables(length_row, id_row, adapter_slot, local_pos):
    ends = jnp.cumsum(length_row)
    starts = ends - length_row
    prompt = jnp.sum((ends[None, :] <= local_pos[:, None]).astype(jnp.int32), axis=1)
    onehot = (prompt[:, None] == jnp.arange(length_row.shape[0])[None, :]).astype(jnp.int32)
    position = local_pos - jnp.sum(onehot * starts[None, :], axis=1)
    adapter = jnp.sum(onehot * id_row[None, :], axis=1)
    slot_hot = (adapter[:, None] == jnp.arange(adapter_slot.shape[0])[None, :]).astype(jnp.int32)
    slot = jnp.sum(slot_hot * adapter_slot[None, :], axis=1)
    return (prompt, position, adapter, slot)


def swap(values):
    return lax.ppermute(values, "narrow", perm=[(0, 1), (1, 0)])


def body(
    tokens,
    attn_gain,
    q_weight,
    kva_weight,
    kv_gain,
    kvb_weight,
    o_weight,
    adapter_down,
    adapter_up_weight,
    lengths,
    adapter_ids,
    adapter_slot,
):
    rows = tokens.shape[0]
    half_width = tokens.shape[1]
    heads_here = o_weight.shape[0] // VDIM
    prompts_here = lengths.shape[1]
    q_cols = q_weight.shape[1]
    me = lax.axis_index("narrow")
    mine_first = me == 0
    joined = jnp.concatenate([q_weight, kva_weight], axis=1)
    joined = lax.all_gather(joined, "wide", axis=0, tiled=True)
    other = swap(tokens)
    whole = jnp.concatenate(
        [jnp.where(mine_first, tokens, other), jnp.where(mine_first, other, tokens)], axis=1
    )
    slots_here = adapter_down.shape[1] // RANK
    prompt_ids = adapter_ids[0]
    id_hot = (prompt_ids[:, None] == jnp.arange(adapter_slot.shape[0])[None, :]).astype(jnp.int32)
    prompt_slot = jnp.sum(id_hot * adapter_slot[None, :], axis=1)
    owner = prompt_slot // slots_here
    local_slot = prompt_slot % slots_here
    picked = jnp.concatenate(
        [
            lax.dynamic_slice_in_dim(adapter_down, local_slot[p] * RANK, RANK, 1)
            for p in range(prompts_here)
        ],
        axis=1,
    )
    picked_other = swap(picked)
    own_block = jnp.repeat(owner == me, RANK)
    chosen = jnp.where(own_block[None, :], picked, picked_other)
    normed = rms_scale(whole.astype(jnp.float32), attn_gain).astype(jnp.bfloat16)
    local_pos = jnp.arange(rows)
    prompt, position, adapter, slot = token_tables(
        lengths[0], adapter_ids[0], adapter_slot, local_pos
    )
    projections = jnp.dot(normed, joined, preferred_element_type=jnp.float32)
    query_vectors = projections[:, :q_cols]
    kv_pre = projections[:, q_cols:]
    member = (prompt[:, None] == jnp.arange(prompts_here)[None, :]).astype(jnp.float32)
    low = jnp.dot(normed, chosen, preferred_element_type=jnp.float32).reshape(
        rows, prompts_here, RANK
    )
    lowrank = jnp.sum(low * member[:, :, None], axis=1).astype(jnp.bfloat16)
    up_blocks = [
        lax.dynamic_slice_in_dim(adapter_up_weight, prompt_ids[prompt_index] * RANK, RANK, 0)
        for prompt_index in range(prompts_here)
    ]
    up_weight_rows = jnp.concatenate(up_blocks, axis=0)
    spread_rows = (member.astype(jnp.bfloat16)[:, :, None] * lowrank[:, None, :]).reshape(
        rows, prompts_here * RANK
    )
    query_vectors = query_vectors + ADAPTER_SCALE * jnp.dot(
        spread_rows, up_weight_rows, preferred_element_type=jnp.float32
    )
    query_vectors = query_vectors.reshape(rows, heads_here, NOPE + ROPE)
    query_vectors = jnp.concatenate(
        [query_vectors[..., :NOPE], rotate(query_vectors[..., NOPE:], position)], axis=-1
    ).astype(jnp.bfloat16)
    latent = rms_scale(kv_pre[:, :LATENT], kv_gain).astype(jnp.bfloat16)
    key_rope = rotate(kv_pre[:, LATENT:], position).astype(jnp.bfloat16)
    latent_cache = jnp.concatenate([latent, key_rope], axis=1)
    expanded = jnp.dot(latent, kvb_weight, preferred_element_type=jnp.float32).astype(jnp.bfloat16)
    expanded = expanded.reshape(rows, heads_here, NOPE + VDIM)
    key_nope = expanded[..., :NOPE]
    values = expanded[..., NOPE:]
    scale = 1.0 / jnp.sqrt(jnp.float32(NOPE + ROPE))
    scores = jnp.einsum(
        "qhd,khd->hqk", query_vectors[..., :NOPE], key_nope, preferred_element_type=jnp.float32
    )
    scores = scores + jnp.einsum(
        "qhd,kd->hqk", query_vectors[..., NOPE:], key_rope, preferred_element_type=jnp.float32
    )
    scores = scores * scale
    allowed = (prompt[None, :] == prompt[:, None]) & (local_pos[None, :] <= local_pos[:, None])
    scores = jnp.where(allowed[None, :, :], scores, jnp.float32(-1e30))
    top = jnp.max(scores, axis=-1, keepdims=True)
    expo = jnp.exp(scores - top)
    weights = (expo / jnp.sum(expo, axis=-1, keepdims=True)).astype(jnp.bfloat16)
    attended = jnp.einsum(
        "hqk,khd->qhd", weights, values, preferred_element_type=jnp.float32
    ).astype(jnp.bfloat16)
    attended = attended.reshape(rows, heads_here * VDIM)
    their_cols = lax.dynamic_slice_in_dim(o_weight, (1 - me) * half_width, half_width, 1)
    my_cols = lax.dynamic_slice_in_dim(o_weight, me * half_width, half_width, 1)
    theirs = jnp.dot(attended, their_cols, preferred_element_type=jnp.float32).astype(jnp.bfloat16)
    received = swap(theirs)
    mine = jnp.dot(attended, my_cols, preferred_element_type=jnp.float32).astype(jnp.bfloat16)
    projected = mine.astype(jnp.float32) + received.astype(jnp.float32)
    hidden = (tokens.astype(jnp.float32) + projected).astype(jnp.bfloat16)
    return (hidden, latent_cache)


def solution(mesh):
    return jax.shard_map(
        body,
        mesh=mesh,
        in_specs=(
            P("wide", "narrow"),
            P(),
            P("wide", "narrow"),
            P("wide", None),
            P(),
            P(None, "narrow"),
            P("narrow", None),
            P(None, "narrow"),
            P(None, "narrow"),
            P("wide", None),
            P("wide", None),
            P(),
        ),
        out_specs=(P("wide", "narrow"), P("wide", None)),
        check_vma=False,
    )
```

profile of v0, /device:TPU:1, one launch (start us, length us, event | category | flops | bytes accessed | tf_op | source)
XLA Modules:
  0.0 205.4 jit_solution(6438729907557349726)
XLA Ops:
  7.2 0.0 copy-start
  7.2 0.0 copy-start.9
  7.2 0.0 all-gather.2.cloned.1.call-start
  7.3 1.7 pad_maximum_fusion.3
  9.0 0.0 all-gather.2.cloned.1.call-update
  9.0 1.5 collective-permute-start
  10.5 0.9 select_reduce_fusion.1
  11.4 0.6 fusion.51
  14.4 2.5 %constant_dynamic-slice_fusion.7 = (bf16[2048,16]{1,0:T(8,128)(2,1)S(1)}, bf16[2048,16]{1,0:T(8,128)(2,1)S(1)}, bf16[2048,16]{1,0:T(8,128)(2,1)S(1)}, bf16[2048,16]{1,0:T(8,128)(2,1)S(1)}) fusion(bf16[2048,512]{1,0:T(8,128)(2,1)} %param.19, s32[]{:T(128)S(6)} %select_n.67, s32[]{:T(128)S(6)} %select_n.68, s32[]{:T(128)S(6)} %select_n.70, s32[]{:T(128)S(6)} %select_n.69), kind=kLoop, calls=%fused_computation.76 | loop fusion | bytes 524304 | tf_op jit(solution)/shard_map/dynamic_slice | solution.py:88
  16.9 1.5 pad_maximum_fusion.2
  18.4 0.0 collective-permute-start.1
  18.4 0.6 fusion.50
  21.5 0.1 broadcast_in_dim.21
  21.5 0.1 broadcast_in_dim.22
  21.6 0.2 reduce-window.4
  21.8 0.6 multiply_exponential_fusion
  22.4 0.1 convert_reduce_fusion
  22.5 0.1 select_reduce_fusion
  22.6 0.6 subtract_convert_fusion.2
  23.2 1.5 constant_dynamic-slice_fusion.3
  24.7 0.6 fusion.7
  25.3 2.5 %broadcast_select_fusion.1 = (bf16[1024,1024]{1,0:T(8,128)(2,1)S(1)}, bf16[1024,1024]{1,0:T(8,128)(2,1)S(1)}) fusion(bf16[1024,1024]{1,0:T(8,128)(2,1)} %param.12, bf16[1024,1024]{1,0:T(8,128)(2,1)} %collective-permute-done, pred[]{:T(512)S(6)} %eq.70), kind=kLoop, calls=%fused_computation.28 | loop fusion | flops 2097152 | bytes 8388609 | tf_op jit(solution)/shard_map/jit(_where)/select_n | solution.py:78
  27.8 0.0 copy-start.4
  27.8 1.0 fusion.4
  28.8 0.0 collective-permute-done.1
  28.8 3.1 %fusion.26 = f32[1024,64]{0,1:T(8,128)S(1)} fusion(bf16[2048,64]{1,0:T(8,128)(2,1)} %pad_maximum_fusion.2, bf16[2048,64]{1,0:T(8,128)(2,1)} %collective-permute-done.1, pred[64]{0:T(512)(128)(4,1)S(1)} %broadcast_in_dim.22, f32[2048]{0:T(1024)S(1)} %convert_element_type.94, f32[1024]{0:T(1024)S(1)} %add_rsqrt_fusion.1, ...), kind=kOutput, calls=%fused_computation.39 | convolution fusion | flops 283246592 | bytes 4993088 | tf_op jit(solution)/shard_map/dot_general | solution.py:105
  32.1 62.5 %all-gather.2.cloned.1.call-done = bf16[2048,2112]{1,0:T(8,128)(2,1)} async-done(((bf16[32,2112]{1,0:T(8,128)(2,1)}), bf16[2048,2112]{1,0:T(8,128)(2,1)}) %all-gather.2.cloned.1.call-update) | async-done | bytes 8650768 | tf_op jit(solution)/shard_map/all_gather | solution.py:75
  94.6 16.1 %fusion.47 = f32[1024,2112]{0,1:T(8,128)} fusion(bf16[2048,2112]{1,0:T(8,128)(2,1)} %all-gather.2.cloned.1.call-done, f32[2048]{0:T(1024)S(1)} %convert_element_type.94, f32[1024]{0:T(1024)S(1)} %add_rsqrt_fusion.1, bf16[1024,1024]{1,0:T(8,128)(2,1)} %copy-done.4, bf16[1024,1024]{1,0:T(8,128)(2,1)} %copy-done.3), kind=kOutput, calls=%fused_computation.91 | convolution fusion | flops 8873050112 | bytes 21508096 | tf_op jit(solution)/shard_map/dot_general | solution.py:101
  110.7 1.8 multiply_reduce_fusion
  112.4 1.8 multiply_convert_fusion
  114.3 0.0 copy-start.5
  114.3 2.4 %convolution_convert_fusion = bf16[1024,2048]{1,0:T(8,128)(2,1)S(1)} fusion(bf16[1024,512]{0,1:T(8,128)(2,1)S(1)} %multiply_convert_fusion, bf16[512,2048]{1,0:T(8,128)(2,1)S(1)} %copy-done), kind=kOutput, calls=%fused_computation.18 | convolution fusion | flops 2149580800 | bytes 7340032 | tf_op jit(solution)/shard_map/dot_general | solution.py:127
  116.7 0.0 slice-start
  116.7 1.5 copy.40
  118.3 1.6 fusion.49
  119.9 1.5 slice-done.2
  121.4 0.6 subtract_convert_fusion.1
  121.9 1.0 slice_add_fusion
  123.0 2.7 %copy-done.2 = f32[1024,1536]{0,1:T(8,128)} copy-done((f32[1024,1536]{0,1:T(8,128)}, f32[1024,1536]{0,1:T(8,128)S(1)}, u32[]{:S(2)}) %copy-start.2) | copy-done | bytes 6291480
  125.7 0.3 subtract_convert_fusion
  126.0 13.2 %fusion.22 = f32[1024,1024,8]{1,0,2:T(8,128)} fusion(bf16[1024,8,32]{0,2,1:T(8,128)(2,1)S(1)} %get-tuple-element.5, bf16[1024,8,32]{0,2,1:T(8,128)(2,1)S(1)} %get-tuple-element.4, bf16[1024,32]{0,1:T(8,128)(2,1)S(1)} %get-tuple-element.3, bf16[1024,32]{0,1:T(8,128)(2,1)S(1)} %get-tuple-element.2), kind=kOutput, calls=%fused_computation.32 | convolution fusion | flops 1076101120 | bytes 34734080 | tf_op jit(solution)/shard_map/qhd,kd->hqk/dot_general | solution.py:135
  139.2 26.8 %fusion.52 = (f32[8,1024]{1,0:T(8,128)S(1)}, f32[8,1024,1024]{1,2,0:T(8,128)}) fusion(f32[1024,1024,8]{1,0,2:T(8,128)} %fusion.22, pred[1024,1024]{0,1:T(8,128)(4,1)S(1)} %fusion.7, f32[1024,8,192]{0,2,1:T(8,128)} %bitcast.43, bf16[1024,8,128]{2,1,0:T(8,128)(2,1)S(1)} %get-tuple-element.7), kind=kOutput, calls=%fused_computation.95 | convolution fusion | flops 2189427712 | bytes 72384512 | tf_op jit(solution)/shard_map/sub | solution.py:142
  166.0 14.1 %fusion.17 = bf16[8,128,1024]{2,1,0:T(8,128)(2,1)} fusion(f32[8,1024,1024]{1,2,0:T(8,128)} %get-tuple-element.31, f32[8,1024]{1,0:T(8,128)S(1)} %get-tuple-element.30, bf16[1024,8,128]{2,1,0:T(8,128)(2,1)} %get-tuple-element.6), kind=kOutput, calls=%fused_computation.30 | convolution fusion | flops 2165309440 | bytes 37781504 | tf_op jit(solution)/shard_map/hqk,khd->qhd/dot_general | solution.py:144
  180.1 6.0 %fusion.14 = bf16[1024,1024]{1,0:T(8,128)(2,1)} fusion(bf16[1024,1024]{0,1:T(8,128)(2,1)} %bitcast.53, bf16[1024,2048]{1,0:T(8,128)(2,1)} %param.18, s32[]{:T(128)S(6)} %select_n.78), kind=kOutput, calls=%fused_computation.29 | convolution fusion | flops 2148532224 | bytes 6291460 | tf_op jit(solution)/shard_map/dot_general | solution.py:150
  186.1 0.7 collective-permute-start.2
  186.8 1.1 pad_maximum_fusion.1
  187.9 3.0 %collective-permute-done.2 = bf16[1024,1024]{1,0:T(8,128)(2,1)} collective-permute-done((bf16[1024,1024]{1,0:T(8,128)(2,1)}, bf16[1024,1024]{1,0:T(8,128)(2,1)}, u32[]{:S(2)}, u32[]{:S(2)}) %collective-permute-start.2) | collective-permute-done | bytes 2097184 | tf_op jit(solution)/shard_map/ppermute | solution.py:50
  191.0 7.6 %add_convert_fusion = bf16[1024,1024]{1,0:T(8,128)(2,1)} fusion(bf16[1024,1024]{1,0:T(8,128)(2,1)} %collective-permute-done.2, bf16[1024,1024]{1,0:T(8,128)(2,1)} %param.12, bf16[1024,1024]{0,1:T(8,128)(2,1)} %bitcast.54, bf16[1024,2048]{1,0:T(8,128)(2,1)} %param.18, s32[]{:T(128)S(6)} %select_n.77), kind=kOutput, calls=%fused_computation.15 | convolution fusion | flops 2154823680 | bytes 10485764 | tf_op jit(solution)/shard_map/dot_general | solution.py:152
  (39 shorter events, 0.2 us)
Async XLA Ops:
  7.2 107.1 %copy-start = (bf16[512,2048]{1,0:T(8,128)(2,1)S(1)}, bf16[512,2048]{1,0:T(8,128)(2,1)}, u32[]{:S(2)}) copy-start(bf16[512,2048]{1,0:T(8,128)(2,1)} %param.17) | copy-start | bytes 6291460
  7.2 11.2 %copy-start.9 = (s32[1,4]{1,0:T(1,128)S(1)}, s32[1,4]{1,0:T(1,128)}, u32[]{:S(2)}) copy-start(s32[1,4]{1,0:T(1,128)} %param.22) | copy-start | bytes 52
  7.2 14.4 %copy-start.10 = (bf16[2048]{0:T(1024)(128)(2,1)S(1)}, bf16[2048]{0:T(1024)(128)(2,1)}, u32[]{:S(2)}) copy-start(bf16[2048]{0:T(1024)(128)(2,1)} %param.13) | copy-start | bytes 12292
  7.2 14.4 %copy-start.13 = (s32[1,4]{1,0:T(1,128)S(1)}, s32[1,4]{1,0:T(1,128)}, u32[]{:S(2)}) copy-start(s32[1,4]{1,0:T(1,128)} %param.21) | copy-start | bytes 52
  7.2 14.6 %copy-start.11 = (bf16[512]{0:T(512)(128)(2,1)S(1)}, bf16[512]{0:T(512)(128)(2,1)}, u32[]{:S(2)}) copy-start(bf16[512]{0:T(512)(128)(2,1)} %param.16) | copy-start | bytes 3076
  7.2 87.3 %all-gather.2.cloned.1.call-start = ((), (), s32[]{:S(2)}) async-start(), calls=%async_computation | async-start | bytes 9052160 | tf_op jit(solution)/shard_map/all_gather | solution.py:75
  9.0 16.3 %collective-permute-start = (bf16[1024,1024]{1,0:T(8,128)(2,1)}, bf16[1024,1024]{1,0:T(8,128)(2,1)}, u32[]{:S(2)}, u32[]{:S(2)}) collective-permute-start(bf16[1024,1024]{1,0:T(8,128)(2,1)} %param.12), channel_id=1, source_target_pairs={{0,1},{1,0},{2,3},{3,2},{4,5},{5,4},{6,7},{7,6},{8,9},{9,8},{10,11... | collective-permute-start | bytes 6291464 | tf_op jit(solution)/shard_map/ppermute | solution.py:50
  18.4 10.5 %collective-permute-start.1 = (bf16[2048,64]{1,0:T(8,128)(2,1)}, bf16[2048,64]{1,0:T(8,128)(2,1)}, u32[]{:S(2)}, u32[]{:S(2)}) collective-permute-start(bf16[2048,64]{1,0:T(8,128)(2,1)} %pad_maximum_fusion.2), channel_id=1, source_target_pairs={{0,1},{1,0},{2,3},{3,2},{4,5},{5,4},{6,7},{7,6},{8,9},{9,8},{10,11... | collective-permute-start | bytes 786440 | tf_op jit(solution)/shard_map/ppermute | solution.py:50
  27.8 4.2 %copy-start.3 = (bf16[1024,1024]{1,0:T(8,128)(2,1)}, bf16[1024,1024]{1,0:T(8,128)(2,1)S(1)}, u32[]{:S(2)}) copy-start(bf16[1024,1024]{1,0:T(8,128)(2,1)S(1)} %get-tuple-element.8) | copy-start | bytes 6291460
  27.8 4.2 %copy-start.4 = (bf16[1024,1024]{1,0:T(8,128)(2,1)}, bf16[1024,1024]{1,0:T(8,128)(2,1)S(1)}, u32[]{:S(2)}) copy-start(bf16[1024,1024]{1,0:T(8,128)(2,1)S(1)} %get-tuple-element.9) | copy-start | bytes 6291460
  114.3 2.4 %copy-start.5 = (bf16[1024,512]{0,1:T(8,128)(2,1)}, bf16[1024,512]{0,1:T(8,128)(2,1)S(1)}, u32[]{:S(2)}) copy-start(bf16[1024,512]{0,1:T(8,128)(2,1)S(1)} %multiply_convert_fusion) | copy-start | bytes 3145732
  116.7 3.2 %slice-start = ((s8[8650752]{0:T(1024)(128)(4,1)}), s8[262144]{0:T(1024)(128)(4,1)S(1)}, s32[]{:S(2)}) async-start(s8[8650752]{0:T(1024)(128)(4,1)} %bitcast.44), calls=%async_computation.1 | async-start | bytes 524288
  116.7 3.2 %slice-start.1 = ((s8[8650752]{0:T(1024)(128)(4,1)}), s8[4194304]{0:T(1024)(128)(4,1)S(1)}, s32[]{:S(2)}) async-start(s8[8650752]{0:T(1024)(128)(4,1)} %bitcast.44), calls=%async_computation.2 | async-start | bytes 8388608
  118.2 3.1 %slice-start.2 = ((s8[8650752]{0:T(1024)(128)(4,1)}), s8[4194304]{0:T(1024)(128)(4,1)S(1)}, s32[]{:S(2)}) async-start(s8[8650752]{0:T(1024)(128)(4,1)} %bitcast.44), calls=%async_computation.3 | async-start | bytes 8388608
  118.2 3.1 %copy-start.8 = (f32[1024]{0:T(1024)S(1)}, f32[1024]{0:T(1024)}, u32[]{:S(2)}) copy-start(f32[1024]{0:T(1024)} %subtract_convert_fusion.2) | copy-start | bytes 12292
  118.2 3.1 %copy-start.12 = (f32[32]{0:T(128)S(1)}, f32[32]{0:T(128)}, u32[]{:S(2)}) copy-start(f32[32]{0:T(128)} %multiply_exponential_fusion) | copy-start | bytes 388
  118.3 3.7 %copy-start.7 = (bf16[16,1536]{1,0:T(8,128)(2,1)S(1)}, bf16[16,1536]{1,0:T(8,128)(2,1)}, u32[]{:S(2)}) copy-start(bf16[16,1536]{1,0:T(8,128)(2,1)} %get-tuple-element.13) | copy-start | bytes 147460
  123.0 2.7 %copy-start.2 = (f32[1024,1536]{0,1:T(8,128)}, f32[1024,1536]{0,1:T(8,128)S(1)}, u32[]{:S(2)}) copy-start(f32[1024,1536]{0,1:T(8,128)S(1)} %slice_add_fusion) | copy-start | bytes 18874372
  180.1 6.7 %copy-start.6 = (bf16[1024,512]{0,1:T(8,128)(2,1)S(1)}, bf16[1024,512]{0,1:T(8,128)(2,1)}, u32[]{:S(2)}) copy-start(bf16[1024,512]{0,1:T(8,128)(2,1)} %copy-done.5) | copy-start | bytes 3145732
  186.1 4.8 %collective-permute-start.2 = (bf16[1024,1024]{1,0:T(8,128)(2,1)}, bf16[1024,1024]{1,0:T(8,128)(2,1)}, u32[]{:S(2)}, u32[]{:S(2)}) collective-permute-start(bf16[1024,1024]{1,0:T(8,128)(2,1)} %fusion.14), channel_id=1, source_target_pairs={{0,1},{1,0},{2,3},{3,2},{4,5},{5,4},{6,7},{7,6},{8,9},{9,8},{10,11... | collective-permute-start | bytes 6291464 | tf_op jit(solution)/shard_map/ppermute | solution.py:50
  191.0 7.6 %copy-start.1 = (bf16[512,2048]{1,0:T(8,128)(2,1)S(1)}, bf16[512,2048]{1,0:T(8,128)(2,1)}, u32[]{:S(2)}) copy-start(bf16[512,2048]{1,0:T(8,128)(2,1)} %param.17) | copy-start | bytes 6291460
Sparse Core Ops, SparseCore 0:
  10.8 83.6 all-gather.1
where the time goes:
time: 206 us; the launch traced here: 205 us
  matrix products  90.3 us (44%)
  waiting for transfers between devices  65.6 us (32%)
  between operations  19.2 us (9%)
  other arithmetic  15.3 us (7%)
  local copies, waits for them, and re-layouts  12.7 us (6%)
  starting transfers between devices  2.24 us (1%)
    all_gather x1, waiting for transfers between devices, body(): joined = lax.all_gather(joined, 'wide', axis=0, tiled=True)  62.5 us
    sub x1, matrix products, body(): expo = jnp.exp(scores - top)  26.8 us
    dot_general x1, matrix products, body(): projections = jnp.dot(normed, joined, preferred_element_type=jnp.float32)  16.1 us
    dot_general x1, matrix products, body(): jnp.einsum('hqk,khd->qhd', weights, values, preferred_element_type=jnp.fl...  14.1 us
    dot_general x1, matrix products, body(): jnp.einsum('qhd,kd->hqk', query_vectors[..., NOPE:], key_rope, preferred_...  13.2 us
    dot_general x1, matrix products, body(): jnp.dot(attended, my_cols, preferred_element_type=jnp.float32)  7.56 us
    dot_general x1, matrix products, body(): jnp.dot(attended, their_cols, preferred_element_type=jnp.float32)  6.02 us
    unnamed x35, local copies, waits for them, and re-layouts  5.77 us
  transfers between devices with their start and end apart: 4, of which 2 were waited for; matrix products, arithmetic and copies ran while one was open for 9% of the time, Pallas kernels for 0%

commit v1 on v0

--- a/solution.py
+++ b/solution.py
@@ -72,7 +72,9 @@
     me = lax.axis_index("narrow")
     mine_first = me == 0
     joined = jnp.concatenate([q_weight, kva_weight], axis=1)
-    joined = lax.all_gather(joined, "wide", axis=0, tiled=True)
+    joined = jnp.concatenate(
+        lax.all_to_all(jnp.stack([joined] * lax.axis_size("wide")), "wide", 0, 0), axis=0
+    )
     other = swap(tokens)
     whole = jnp.concatenate(
         [jnp.where(mine_first, tokens, other), jnp.where(mine_first, other, tokens)], axis=1

time: 206 us -> 255 us (1.24)
  the two profiles are of different devices: /device:TPU:1 before, /device:TPU:5 now
where the time goes in v1:
time: 255 us
  waiting for transfers between devices  114 us (45%)
  matrix products  90.3 us (35%)
  local copies, waits for them, and re-layouts  16.5 us (6%)
  starting transfers between devices  14.2 us (6%)
  other arithmetic  13.9 us (5%)
  between operations  5.87 us (2%)
    all_to_all x1, waiting for transfers between devices, body(): lax.all_to_all(jnp.stack([joined] * lax.axis_size('wide')), 'wide', 0, 0)  111 us
    sub x1, matrix products, body(): expo = jnp.exp(scores - top)  26.8 us
    dot_general x1, matrix products, body(): projections = jnp.dot(normed, joined, preferred_element_type=jnp.float32)  16.1 us
    dot_general x1, matrix products, body(): jnp.einsum('hqk,khd->qhd', weights, values, preferred_element_type=jnp.fl...  14.1 us
    dot_general x1, matrix products, body(): jnp.einsum('qhd,kd->hqk', query_vectors[..., NOPE:], key_rope, preferred_...  13.2 us
    all_to_all x1, starting transfers between devices, body(): lax.all_to_all(jnp.stack([joined] * lax.axis_size('wide')), 'wide', 0, 0)  11.2 us
    dot_general x1, matrix products, body(): jnp.dot(attended, my_cols, preferred_element_type=jnp.float32)  7.56 us
    dot_general x1, matrix products, body(): jnp.dot(attended, their_cols, preferred_element_type=jnp.float32)  6.02 us
  transfers between devices with their start and end apart: 4, of which 2 were waited for; matrix products, arithmetic and copies ran while one was open for 7% of the time, Pallas kernels for 0%

profile of v1, /device:TPU:5, one launch (start us, length us, event | category | flops | bytes accessed | tf_op | source)
XLA Modules:
  0.0 254.8 jit_solution(3985171504306650388)
XLA Ops:
  0.6 0.0 copy-start
  0.6 1.1 pad_maximum_fusion.3
  1.7 4.0 %stack.2 = bf16[64,32,2112]{2,1,0:T(8,128)(2,1)} broadcast(bf16[32,2112]{1,0:T(8,128)(2,1)S(1)} %pad_maximum_fusion.3), dimensions={1,2} | broadcast | bytes 8785920 | tf_op jit(solution)/shard_map/stack | solution.py:76
  5.8 11.2 %all-to-all-start = ((bf16[64,32,2112]{2,1,0:T(8,128)(2,1)}), bf16[64,32,2112]{2,1,0:T(8,128)(2,1)}, u32[]{:S(2)}, u32[]{:S(2)}) async-start(bf16[64,32,2112]{2,1,0:T(8,128)(2,1)} %stack.2), calls=%async_computation | async-start | bytes 17825792 | tf_op jit(solution)/shard_map/all_to_all | solution.py:76
  17.0 0.0 copy-start.10
  17.0 0.0 copy-start.14
  17.0 0.0 copy-start.11
  17.0 1.3 collective-permute-start
  18.3 0.2 select_reduce_fusion.1
  18.5 0.6 fusion.51
  21.7 2.2 constant_dynamic-slice_fusion.7
  23.9 1.5 pad_maximum_fusion.2
  25.4 0.0 collective-permute-start.1
  25.4 0.6 fusion.50
  28.5 0.1 broadcast_in_dim.21
  28.5 0.1 broadcast_in_dim.22
  28.6 0.2 reduce-window.4
  28.8 0.5 multiply_exponential_fusion
  29.3 0.1 convert_reduce_fusion
  29.4 0.1 select_reduce_fusion
  29.5 0.6 subtract_convert_fusion.2
  30.1 1.5 constant_dynamic-slice_fusion.3
  31.6 0.6 fusion.7
  32.2 2.5 broadcast_select_fusion.1
  34.7 0.0 copy-start.4
  34.7 1.0 fusion.4
  35.8 3.1 %fusion.26 = f32[1024,64]{0,1:T(8,128)S(1)} fusion(bf16[2048,64]{1,0:T(8,128)(2,1)} %pad_maximum_fusion.2, bf16[2048,64]{1,0:T(8,128)(2,1)} %collective-permute-done.1, pred[64]{0:T(512)(128)(4,1)S(1)} %broadcast_in_dim.22, f32[2048]{0:T(1024)S(1)} %convert_element_type.94, f32[1024]{0:T(1024)S(1)} %add_rsqrt_fusion.1, ...), kind=kOutput, calls=%fused_computation.39 | convolution fusion | flops 283246592 | bytes 4993088 | tf_op jit(solution)/shard_map/dot_general | solution.py:107
  38.9 111.0 %all-to-all-done = bf16[64,32,2112]{2,1,0:T(8,128)(2,1)} async-done(((bf16[64,32,2112]{2,1,0:T(8,128)(2,1)}), bf16[64,32,2112]{2,1,0:T(8,128)(2,1)}, u32[]{:S(2)}, u32[]{:S(2)}) %all-to-all-start) | async-done | bytes 8650784 | tf_op jit(solution)/shard_map/all_to_all | solution.py:76
  149.9 16.1 %fusion.47 = f32[1024,2112]{0,1:T(8,128)} fusion(bf16[2048,2112]{1,0:T(8,128)(2,1)} %bitcast, f32[2048]{0:T(1024)S(1)} %convert_element_type.94, f32[1024]{0:T(1024)S(1)} %add_rsqrt_fusion.1, bf16[1024,1024]{1,0:T(8,128)(2,1)} %copy-done.4, bf16[1024,1024]{1,0:T(8,128)(2,1)} %copy-done.3), kind=kOutput, calls=%fused_computation.91 | convolution fusion | flops 8873050112 | bytes 21508096 | tf_op jit(solution)/shard_map/dot_general | solution.py:103
  166.0 1.8 multiply_reduce_fusion
  167.8 1.8 multiply_convert_fusion
  169.6 0.0 copy-start.5
  169.6 2.4 convolution_convert_fusion
  172.1 1.5 copy.40
  173.6 1.6 fusion.49
  175.2 1.5 slice-done.2
  176.7 0.6 subtract_convert_fusion.1
  177.3 1.0 slice_add_fusion
  178.4 2.7 %copy-done.2 = f32[1024,1536]{0,1:T(8,128)} copy-done((f32[1024,1536]{0,1:T(8,128)}, f32[1024,1536]{0,1:T(8,128)S(1)}, u32[]{:S(2)}) %copy-start.2) | copy-done | bytes 6291480
  181.0 0.3 subtract_convert_fusion
  181.4 13.2 %fusion.22 = f32[1024,1024,8]{1,0,2:T(8,128)} fusion(bf16[1024,8,32]{0,2,1:T(8,128)(2,1)S(1)} %get-tuple-element.5, bf16[1024,8,32]{0,2,1:T(8,128)(2,1)S(1)} %get-tuple-element.4, bf16[1024,32]{0,1:T(8,128)(2,1)S(1)} %get-tuple-element.3, bf16[1024,32]{0,1:T(8,128)(2,1)S(1)} %get-tuple-element.2), kind=kOutput, calls=%fused_computation.32 | convolution fusion | flops 1076101120 | bytes 34734080 | tf_op jit(solution)/shard_map/qhd,kd->hqk/dot_general | solution.py:137
  194.6 26.8 %fusion.52 = (f32[8,1024]{1,0:T(8,128)S(1)}, f32[8,1024,1024]{1,2,0:T(8,128)}) fusion(f32[1024,1024,8]{1,0,2:T(8,128)} %fusion.22, pred[1024,1024]{0,1:T(8,128)(4,1)S(1)} %fusion.7, f32[1024,8,192]{0,2,1:T(8,128)} %bitcast.44, bf16[1024,8,128]{2,1,0:T(8,128)(2,1)S(1)} %get-tuple-element.7), kind=kOutput, calls=%fused_computation.95 | convolution fusion | flops 2189427712 | bytes 72384512 | tf_op jit(solution)/shard_map/sub | solution.py:144
  221.3 14.1 %fusion.17 = bf16[8,128,1024]{2,1,0:T(8,128)(2,1)} fusion(f32[8,1024,1024]{1,2,0:T(8,128)} %get-tuple-element.31, f32[8,1024]{1,0:T(8,128)S(1)} %get-tuple-element.30, bf16[1024,8,128]{2,1,0:T(8,128)(2,1)} %get-tuple-element.6), kind=kOutput, calls=%fused_computation.30 | convolution fusion | flops 2165309440 | bytes 37781504 | tf_op jit(solution)/shard_map/hqk,khd->qhd/dot_general | solution.py:146
  235.5 6.0 %fusion.14 = bf16[1024,1024]{1,0:T(8,128)(2,1)} fusion(bf16[1024,1024]{0,1:T(8,128)(2,1)} %bitcast.54, bf16[1024,2048]{1,0:T(8,128)(2,1)} %param.18, s32[]{:T(128)S(6)} %select_n.78), kind=kOutput, calls=%fused_computation.29 | convolution fusion | flops 2148532224 | bytes 6291460 | tf_op jit(solution)/shard_map/dot_general | solution.py:152
  241.5 1.7 collective-permute-start.2
  243.1 1.1 pad_maximum_fusion.1
  244.2 3.0 %collective-permute-done.2 = bf16[1024,1024]{1,0:T(8,128)(2,1)} collective-permute-done((bf16[1024,1024]{1,0:T(8,128)(2,1)}, bf16[1024,1024]{1,0:T(8,128)(2,1)}, u32[]{:S(2)}, u32[]{:S(2)}) %collective-permute-start.2) | collective-permute-done | bytes 2097184 | tf_op jit(solution)/shard_map/ppermute | solution.py:50
  247.2 7.6 %add_convert_fusion = bf16[1024,1024]{1,0:T(8,128)(2,1)} fusion(bf16[1024,1024]{1,0:T(8,128)(2,1)} %collective-permute-done.2, bf16[1024,1024]{1,0:T(8,128)(2,1)} %param.12, bf16[1024,1024]{0,1:T(8,128)(2,1)} %bitcast.55, bf16[1024,2048]{1,0:T(8,128)(2,1)} %param.18, s32[]{:T(128)S(6)} %select_n.77), kind=kOutput, calls=%fused_computation.15 | convolution fusion | flops 2154823680 | bytes 10485764 | tf_op jit(solution)/shard_map/dot_general | solution.py:154
  (41 shorter events, 0.2 us)
Async XLA Ops:
  0.6 169.0 %copy-start = (bf16[512,2048]{1,0:T(8,128)(2,1)S(1)}, bf16[512,2048]{1,0:T(8,128)(2,1)}, u32[]{:S(2)}) copy-start(bf16[512,2048]{1,0:T(8,128)(2,1)} %param.17) | copy-start | bytes 6291460
  5.8 12.6 %copy-start.9 = (s32[1,4]{1,0:T(1,128)S(1)}, s32[1,4]{1,0:T(1,128)}, u32[]{:S(2)}) copy-start(s32[1,4]{1,0:T(1,128)} %param.22) | copy-start | bytes 52
  5.8 12.6 %copy-start.13 = (s32[64]{0:T(128)S(1)}, s32[64]{0:T(128)}, u32[]{:S(2)}) copy-start(s32[64]{0:T(128)} %param.23) | copy-start | bytes 772
  5.8 144.1 %all-to-all-start = ((bf16[64,32,2112]{2,1,0:T(8,128)(2,1)}), bf16[64,32,2112]{2,1,0:T(8,128)(2,1)}, u32[]{:S(2)}, u32[]{:S(2)}) async-start(bf16[64,32,2112]{2,1,0:T(8,128)(2,1)} %stack.2), calls=%async_computation | async-start | bytes 17825792 | tf_op jit(solution)/shard_map/all_to_all | solution.py:76
  17.0 11.6 %copy-start.10 = (bf16[2048]{0:T(1024)(128)(2,1)S(1)}, bf16[2048]{0:T(1024)(128)(2,1)}, u32[]{:S(2)}) copy-start(bf16[2048]{0:T(1024)(128)(2,1)} %param.13) | copy-start | bytes 12292
  17.0 11.6 %copy-start.14 = (s32[1,4]{1,0:T(1,128)S(1)}, s32[1,4]{1,0:T(1,128)}, u32[]{:S(2)}) copy-start(s32[1,4]{1,0:T(1,128)} %param.21) | copy-start | bytes 52
  17.0 11.8 %copy-start.11 = (bf16[512]{0:T(512)(128)(2,1)S(1)}, bf16[512]{0:T(512)(128)(2,1)}, u32[]{:S(2)}) copy-start(bf16[512]{0:T(512)(128)(2,1)} %param.16) | copy-start | bytes 3076
  17.0 15.2 %collective-permute-start = (bf16[1024,1024]{1,0:T(8,128)(2,1)}, bf16[1024,1024]{1,0:T(8,128)(2,1)}, u32[]{:S(2)}, u32[]{:S(2)}) collective-permute-start(bf16[1024,1024]{1,0:T(8,128)(2,1)} %param.12), channel_id=1, source_target_pairs={{0,1},{1,0},{2,3},{3,2},{4,5},{5,4},{6,7},{7,6},{8,9},{9,8},{10,11... | collective-permute-start | bytes 6291464 | tf_op jit(solution)/shard_map/ppermute | solution.py:50
  25.4 10.4 %collective-permute-start.1 = (bf16[2048,64]{1,0:T(8,128)(2,1)}, bf16[2048,64]{1,0:T(8,128)(2,1)}, u32[]{:S(2)}, u32[]{:S(2)}) collective-permute-start(bf16[2048,64]{1,0:T(8,128)(2,1)} %pad_maximum_fusion.2), channel_id=1, source_target_pairs={{0,1},{1,0},{2,3},{3,2},{4,5},{5,4},{6,7},{7,6},{8,9},{9,8},{10,11... | collective-permute-start | bytes 786440 | tf_op jit(solution)/shard_map/ppermute | solution.py:50
  34.7 4.1 %copy-start.3 = (bf16[1024,1024]{1,0:T(8,128)(2,1)}, bf16[1024,1024]{1,0:T(8,128)(2,1)S(1)}, u32[]{:S(2)}) copy-start(bf16[1024,1024]{1,0:T(8,128)(2,1)S(1)} %get-tuple-element.8) | copy-start | bytes 6291460
  34.7 4.1 %copy-start.4 = (bf16[1024,1024]{1,0:T(8,128)(2,1)}, bf16[1024,1024]{1,0:T(8,128)(2,1)S(1)}, u32[]{:S(2)}) copy-start(bf16[1024,1024]{1,0:T(8,128)(2,1)S(1)} %get-tuple-element.9) | copy-start | bytes 6291460
  169.6 2.4 copy-start.5
  172.0 3.2 %slice-start = ((s8[8650752]{0:T(1024)(128)(4,1)}), s8[262144]{0:T(1024)(128)(4,1)S(1)}, s32[]{:S(2)}) async-start(s8[8650752]{0:T(1024)(128)(4,1)} %bitcast.45), calls=%async_computation.1 | async-start | bytes 524288
  172.1 3.2 %slice-start.1 = ((s8[8650752]{0:T(1024)(128)(4,1)}), s8[4194304]{0:T(1024)(128)(4,1)S(1)}, s32[]{:S(2)}) async-start(s8[8650752]{0:T(1024)(128)(4,1)} %bitcast.45), calls=%async_computation.2 | async-start | bytes 8388608
  173.6 3.1 %slice-start.2 = ((s8[8650752]{0:T(1024)(128)(4,1)}), s8[4194304]{0:T(1024)(128)(4,1)S(1)}, s32[]{:S(2)}) async-start(s8[8650752]{0:T(1024)(128)(4,1)} %bitcast.45), calls=%async_computation.3 | async-start | bytes 8388608
  173.6 3.1 %copy-start.8 = (f32[1024]{0:T(1024)S(1)}, f32[1024]{0:T(1024)}, u32[]{:S(2)}) copy-start(f32[1024]{0:T(1024)} %subtract_convert_fusion.2) | copy-start | bytes 12292
  173.6 3.1 %copy-start.12 = (f32[32]{0:T(128)S(1)}, f32[32]{0:T(128)}, u32[]{:S(2)}) copy-start(f32[32]{0:T(128)} %multiply_exponential_fusion) | copy-start | bytes 388
  173.6 3.7 %copy-start.7 = (bf16[16,1536]{1,0:T(8,128)(2,1)S(1)}, bf16[16,1536]{1,0:T(8,128)(2,1)}, u32[]{:S(2)}) copy-start(bf16[16,1536]{1,0:T(8,128)(2,1)} %get-tuple-element.13) | copy-start | bytes 147460
  178.4 2.7 %copy-start.2 = (f32[1024,1536]{0,1:T(8,128)}, f32[1024,1536]{0,1:T(8,128)S(1)}, u32[]{:S(2)}) copy-start(f32[1024,1536]{0,1:T(8,128)S(1)} %slice_add_fusion) | copy-start | bytes 18874372
  235.4 7.7 %copy-start.6 = (bf16[1024,512]{0,1:T(8,128)(2,1)S(1)}, bf16[1024,512]{0,1:T(8,128)(2,1)}, u32[]{:S(2)}) copy-start(bf16[1024,512]{0,1:T(8,128)(2,1)} %copy-done.5) | copy-start | bytes 3145732
  241.5 5.8 %collective-permute-start.2 = (bf16[1024,1024]{1,0:T(8,128)(2,1)}, bf16[1024,1024]{1,0:T(8,128)(2,1)}, u32[]{:S(2)}, u32[]{:S(2)}) collective-permute-start(bf16[1024,1024]{1,0:T(8,128)(2,1)} %fusion.14), channel_id=1, source_target_pairs={{0,1},{1,0},{2,3},{3,2},{4,5},{5,4},{6,7},{7,6},{8,9},{9,8},{10,11... | collective-permute-start | bytes 6291464 | tf_op jit(solution)/shard_map/ppermute | solution.py:50
  247.2 7.6 %copy-start.1 = (bf16[512,2048]{1,0:T(8,128)(2,1)S(1)}, bf16[512,2048]{1,0:T(8,128)(2,1)}, u32[]{:S(2)}) copy-start(bf16[512,2048]{1,0:T(8,128)(2,1)} %param.17) | copy-start | bytes 6291460
